TPU v7x, 128 devices: a whole 4x4x4 slice. The times are simulated.
128 devices in a mesh: det: 8 (over x, core), tm: 16 (over z, y).
Axes of the slice: x: 4, y: 4, z: 4, core: 2. Of those that a mesh axis runs over, the one named last changes fastest.
Arguments:
- samples: float32 [32, 1024, 128], P('det', 'tm'), may hold values from -6 to 6
- pointing: bfloat16 [32, 1024, 128, 128], P('det', 'tm'), may hold values from -0.25 to 0.25
- pix_block: int32 [32, 1024], P('det', 'tm'), may hold values from 0 to 8191, as said below
- det_weight: float32 [32], P('det'), may hold values from 0.5 to 2
- start_map: float32 [128, 8192], P(('det', 'tm')), may hold values from -6 to 6
- legendre: bfloat16 [1024, 6144, 128], P(('det', 'tm')), may hold values from -0.5 to 0.5
- prior_gain: float32 [6144], replicated, may hold values from 0.3 to 3
- m_values: int32 [1024], replicated, may hold values from 0 to 4095, as said below
- cycle_offset: int32 [128], P(('det', 'tm')), may hold values from 0 to 8191
Outputs:
- final_map: float32 [128, 8192], P(('det', 'tm'))
Inputs may be any that keep to these rules, and one draw needn't show every extreme that they name: `m_values`: strictly increasing; entry k lies in k * 4 to (k + 1) * 4 - 1, the first is 0 and the last is 4095. `pix_block`: the cycle owner of block b is the device holding cycle b // 64 of the map; among the 4 x 64 sample blocks of one device, at most 8 name blocks of any one owner, and on every device some owner gets exactly 8.
All inputs are finite; a program needn't handle non-finite values.
Results may differ from a plain program's by a relative error of at most 0.0042.
Values may be sent and summed in bfloat16 or wider, within the bound.
No kernel may reach another device: no remote copies, remote signals or barrier semaphores. Data moves between devices by JAX's collectives and lax.ppermute only.
A program may use at most 128 MiB of HBM per device.

v0:
```python
import math
import jax
import jax.numpy as jnp
from jax import lax
from jax.sharding import PartitionSpec as P

ITERS = 2
highest = lax.Precision.HIGHEST


def phase_pair(first_len, second_len, length, sign):
    first = jnp.arange(first_len, dtype=jnp.int32)[:, None]
    second = jnp.arange(second_len, dtype=jnp.int32)[None, :]
    phases = (first * second % length).astype(jnp.float32) * (sign * 2.0 * math.pi / length)
    return (jnp.cos(phases), jnp.sin(phases))


def forward_cycles(field):
    cycles, length = field.shape
    outer_len = length // 128
    shaped = field.reshape(cycles, outer_len, 128)
    cos_outer, sin_outer = phase_pair(outer_len, outer_len, outer_len, -1.0)
    part_re = jnp.einsum("mj,rjk->rmk", cos_outer, shaped, precision=highest)
    part_im = jnp.einsum("mj,rjk->rmk", sin_outer, shaped, precision=highest)
    cos_twist, sin_twist = phase_pair(outer_len, 128, length, -1.0)
    twist_re = part_re * cos_twist - part_im * sin_twist
    twist_im = part_re * sin_twist + part_im * cos_twist
    cos_inner, sin_inner = phase_pair(128, 128, 128, -1.0)
    spec_re = jnp.einsum("rmk,kn->rmn", twist_re, cos_inner, precision=highest) - jnp.einsum(
        "rmk,kn->rmn", twist_im, sin_inner, precision=highest
    )
    spec_im = jnp.einsum("rmk,kn->rmn", twist_re, sin_inner, precision=highest) + jnp.einsum(
        "rmk,kn->rmn", twist_im, cos_inner, precision=highest
    )
    return (spec_re.reshape(cycles, length), spec_im.reshape(cycles, length))


def inverse_cycles(spec_re, spec_im):
    cycles, length = spec_re.shape
    outer_len = length // 128
    shaped_re = spec_re.reshape(cycles, outer_len, 128)
    shaped_im = spec_im.reshape(cycles, outer_len, 128)
    cos_inner, sin_inner = phase_pair(128, 128, 128, 1.0)
    inner_re = jnp.einsum("rmn,nk->rmk", shaped_re, cos_inner, precision=highest) - jnp.einsum(
        "rmn,nk->rmk", shaped_im, sin_inner, precision=highest
    )
    inner_im = jnp.einsum("rmn,nk->rmk", shaped_re, sin_inner, precision=highest) + jnp.einsum(
        "rmn,nk->rmk", shaped_im, cos_inner, precision=highest
    )
    cos_twist, sin_twist = phase_pair(outer_len, 128, length, 1.0)
    twist_re = inner_re * cos_twist - inner_im * sin_twist
    twist_im = inner_re * sin_twist + inner_im * cos_twist
    cos_outer, sin_outer = phase_pair(outer_len, outer_len, outer_len, 1.0)
    field = jnp.einsum("jm,rmk->rjk", cos_outer, twist_re, precision=highest) - jnp.einsum(
        "jm,rmk->rjk", sin_outer, twist_im, precision=highest
    )
    return field.reshape(cycles, length)


def legendre_filter(owned, legendre, prior_gain, m_own):
    count_here, degrees, total_cycles = legendre.shape
    block_rows = min(512, degrees)

    def one_block(index, running):
        start = index * block_rows
        table = lax.dynamic_slice_in_dim(legendre, start, block_rows, 1)
        analysed = jnp.einsum("mlr,cmr->cml", table, owned, preferred_element_type=jnp.float32)
        degree = start + jnp.arange(block_rows, dtype=jnp.int32)
        keep_rows = degree[None, :] >= m_own[:, None]
        gain_block = lax.dynamic_slice_in_dim(prior_gain, start, block_rows)
        scaled = jnp.where(keep_rows[None], analysed * gain_block, 0.0).astype(jnp.bfloat16)
        return running + jnp.einsum(
            "mlr,cml->cmr", table, scaled, preferred_element_type=jnp.float32
        )

    first_block = 0
    initial = jnp.zeros(owned.shape, jnp.float32)
    summed = lax.fori_loop(first_block, degrees // block_rows, one_block, initial)
    return summed * math.sqrt(total_cycles / degrees)


def harmonic_filter(field, legendre, prior_gain, m_values, cycle_offset, m_own):
    cycles_here, length = field.shape
    count = m_values.shape[0]
    outer_len = length // 128
    spectrum_slot = m_values % outer_len * 128 + m_values // outer_len
    spec_re, spec_im = forward_cycles(field)
    pick_re = spec_re[:, spectrum_slot]
    pick_im = spec_im[:, spectrum_slot]
    phases = (m_values[None, :] * cycle_offset[:, None] % length).astype(jnp.float32) * (
        2.0 * math.pi / length
    )
    cos_phase = jnp.cos(phases)
    sin_phase = jnp.sin(phases)
    norm_factor = 1.0 / math.sqrt(length)
    coef_re = (pick_re * cos_phase + pick_im * sin_phase) * norm_factor
    coef_im = (pick_im * cos_phase - pick_re * sin_phase) * norm_factor
    outward = jnp.stack([coef_re.T, coef_im.T]).astype(jnp.bfloat16)
    owned = lax.all_to_all(outward, ("det", "tm"), split_axis=1, concat_axis=2, tiled=True)
    synth = legendre_filter(owned, legendre, prior_gain, m_own)
    returned = lax.all_to_all(synth, ("det", "tm"), split_axis=2, concat_axis=1, tiled=True)
    back_re = returned[0].T
    back_im = returned[1].T
    mode_weight = jnp.where(m_values == 0, 1.0, 2.0).astype(jnp.float32)[None, :]
    harm_re = mode_weight * (back_re * cos_phase - back_im * sin_phase)
    harm_im = mode_weight * (back_re * sin_phase + back_im * cos_phase)
    full_re = jnp.zeros((cycles_here, length), jnp.float32).at[:, spectrum_slot].set(harm_re)
    full_im = jnp.zeros((cycles_here, length), jnp.float32).at[:, spectrum_slot].set(harm_im)
    return inverse_cycles(full_re, full_im) / math.sqrt(2.0 * count)


def on_device(
    samples,
    pointing,
    pix_block,
    det_weight,
    start_map,
    legendre,
    prior_gain,
    m_values,
    cycle_offset,
):
    cycles_here, length = start_map.shape
    per_cycle = length // 128
    owners = lax.axis_size(("det", "tm"))
    total_cycles = cycles_here * owners
    nblocks = total_cycles * per_cycle
    count_here = legendre.shape[0]
    owner_index = lax.axis_index(("det", "tm"))
    m_own = lax.dynamic_slice_in_dim(m_values, owner_index * count_here, count_here)
    flat_pix = pix_block.reshape(-1)
    hit_terms = jnp.broadcast_to(det_weight[:, None], pix_block.shape).reshape(-1)
    hit_local = jnp.zeros((nblocks,), jnp.float32).at[flat_pix].add(hit_terms)
    hit_weight = lax.psum_scatter(
        hit_local.reshape(total_cycles, per_cycle), ("det", "tm"), scatter_dimension=0, tiled=True
    )
    divisor = jnp.repeat(1.0 + 0.25 * hit_weight, 128, axis=1)
    current = start_map
    for iteration in range(ITERS):
        map_half = current.astype(jnp.bfloat16)
        gathered = lax.all_gather(map_half, ("det", "tm"), axis=0, tiled=True).reshape(nblocks, 128)
        picked = gathered[pix_block]
        predicted = jnp.einsum(
            "dtsp,dtp->dts", pointing, picked, preferred_element_type=jnp.float32
        )
        weighted_resid = (det_weight[:, None, None] * (samples - predicted)).astype(jnp.bfloat16)
        binned_terms = jnp.einsum(
            "dtsp,dts->dtp", pointing, weighted_resid, preferred_element_type=jnp.float32
        )
        term_rows = binned_terms.reshape(-1, 128)
        local_map = jnp.zeros((nblocks, 128), jnp.float32).at[flat_pix].add(term_rows)
        local_map = local_map.reshape(total_cycles, length)
        binned = lax.psum_scatter(local_map, ("det", "tm"), scatter_dimension=0, tiled=True)
        filtered = harmonic_filter(current, legendre, prior_gain, m_values, cycle_offset, m_own)
        current = current + (binned - filtered) / divisor
    return current


def solution(mesh):
    placed = (
        P("det", "tm", None),
        P("det", "tm", None, None),
        P("det", "tm"),
        P("det"),
        P(("det", "tm"), None),
        P(("det", "tm"), None, None),
        P(),
        P(),
        P(("det", "tm")),
    )
    return jax.shard_map(
        on_device, mesh=mesh, in_specs=placed, out_specs=P(("det", "tm"), None), check_vma=False
    )
```

profile of v0, /device:TPU:1, one launch (start us, length us, event | category | flops | bytes accessed | tf_op | source)
XLA Modules:
  0.0 604.7 jit_solution(9442821672336099781)
XLA Ops:
  11.7 6.2 %gather_fusion.1 = f32[1024]{0:T(1024)S(1)} fusion(f32[8192]{0:T(1024)S(1)} %fusion.37, s32[1024]{0:T(1024)S(1)} %get-tuple-element.359), kind=kCustom, calls=%fused_computation.1 | custom fusion | bytes 12288 | tf_op jit(solution)/shard_map/gather | solution.py:88
  17.8 6.2 %gather_fusion.2 = f32[1024]{0:T(1024)S(1)} fusion(f32[8192]{0:T(1024)S(1)} %fusion.36, s32[1024]{0:T(1024)S(1)} %get-tuple-element.359), kind=kCustom, calls=%fused_computation.2 | custom fusion | bytes 12288 | tf_op jit(solution)/shard_map/gather | solution.py:89
  25.9 11.5 %all-to-all-start = ((bf16[2,1024,1]{2,0,1:T(2,128)(2,1)}), bf16[2,1024,1]{2,0,1:T(2,128)(2,1)S(1)}, u32[]{:S(2)}, u32[]{:S(2)}) async-start(bf16[2,1024,1]{2,0,1:T(2,128)(2,1)} %copy.46), calls=%async_computation | async-start | bytes 1048576 | tf_op jit(solution)/shard_map/all_to_all | solution.py:99
  40.6 68.5 %all-reduce.1 = f32[128,64]{1,0:T(8,128)S(1)} all-reduce(f32[128,64]{1,0:T(8,128)S(1)} %reshape.520), channel_id=3, replica_groups=mesh['det'=8,'tm'=16] {'det','tm'}, use_global_device_ids=true, to_apply=%region_7.8.clone | all-reduce | flops 8192 | bytes 65536
  109.8 35.5 %while.28 = (s32[]{:T(128)}, f32[2,8,128]{2,0,1:T(2,128)S(1)}, s32[8]{0:T(128)S(1)}, bf16[8,6144,128]{2,1,0:T(8,128)(2,1)}, bf16[2,8,128]{2,0,1:T(2,128)(2,1)S(1...) while((s32[]{:T(128)}, f32[2,8,128]{2,0,1:T(2,128)S(1)}, ...), condition=%wide.region_3.0_spmd.clone, body=%wide.region_2.0_spmd.clone.sunk | while | flops 4227591 | bytes 2137796 | solution.py:78
  145.3 12.6 %reduce = bf16[128,8192]{1,0:T(8,128)(2,1)S(1)} reduce(bf16[128,1,8192]{2,1,0:T(2,128)(2,1)} %all-gather.5.cloned.1.call-done, bf16[]{:T(256)} %constant.249), dimensions={1}, to_apply=%all-gather.reduce_sub_computation | reduce | bytes 4194306 | tf_op jit(solution)/shard_map/all_gather | solution.py:141
  162.9 7.8 %fusion.44 = f32[4,64,1,128]{3,2,1,0:T(1,128)S(1)} fusion(bf16[4,64,128,128]{3,2,1,0:T(8,128)(2,1)} %param.14, bf16[4,64,128,1]{2,1,0,3:T(8,128)(2,1)S(1)} %bitcast.179), kind=kOutput, calls=%fused_computation.73 | convolution fusion | flops 8388608 | bytes 8585216 | tf_op jit(solution)/shard_map/dtsp,dtp->dts/dot_general | solution.py:143
  170.8 5.7 fusion.42
  180.1 4.9 reshape.511
  185.8 4.7 all-to-all-start.1
  190.7 10.1 %all-to-all-done.1 = f32[2,8,128]{1,0,2:T(2,128)S(1)} async-done(((f32[2,8,128]{1,0,2:T(2,128)}), f32[2,8,128]{1,0,2:T(2,128)S(1)}, u32[]{:S(2)}, u32[]{:S(2)}) %all-to-all-start.1) | async-done | bytes 8224 | tf_op jit(solution)/shard_map/all_to_all | solution.py:101
  213.0 123.0 %all-reduce.6.cloned.1.call-done = f32[128,8192]{1,0:T(8,128)} async-done(((f32[128,8192]{1,0:T(8,128)}), f32[128,8192]{1,0:T(8,128)}) %all-reduce.6.cloned.1.call-update) | async-done | bytes 4194320
  339.5 6.2 %gather_fusion.4 = f32[1024]{0:T(1024)S(1)} fusion(f32[8192]{0:T(1024)S(1)} %fusion.34, s32[1024]{0:T(1024)S(1)} %get-tuple-element.359), kind=kCustom, calls=%fused_computation.4 | custom fusion | bytes 12288 | tf_op jit(solution)/shard_map/gather | solution.py:88
  346.8 6.2 %gather_fusion.5 = f32[1024]{0:T(1024)S(1)} fusion(f32[8192]{0:T(1024)S(1)} %fusion.33, s32[1024]{0:T(1024)S(1)} %get-tuple-element.359), kind=kCustom, calls=%fused_computation.5 | custom fusion | bytes 12288 | tf_op jit(solution)/shard_map/gather | solution.py:89
  354.2 6.6 %all-to-all-start.2 = ((bf16[2,1024,1]{2,0,1:T(2,128)(2,1)}), bf16[2,1024,1]{2,0,1:T(2,128)(2,1)S(1)}, u32[]{:S(2)}, u32[]{:S(2)}) async-start(bf16[2,1024,1]{2,0,1:T(2,128)(2,1)} %copy.51), calls=%async_computation.2 | async-start | bytes 1048576 | tf_op jit(solution)/shard_map/all_to_all | solution.py:99
  361.0 13.8 %all-to-all-done.2 = bf16[2,1024,1]{2,0,1:T(2,128)(2,1)S(1)} async-done(((bf16[2,1024,1]{2,0,1:T(2,128)(2,1)}), bf16[2,1024,1]{2,0,1:T(2,128)(2,1)S(1)}, u32[]{:S(2)}, u32[]{:S(2)}) %all-to-all-start.2) | async-done | bytes 4128 | tf_op jit(solution)/shard_map/all_to_all | solution.py:99
  375.4 29.4 %all-gather.7.cloned.1.call-done = bf16[128,1,8192]{2,1,0:T(2,128)(2,1)} async-done(((bf16[1,1,8192]{2,1,0:T(2,128)(2,1)}), bf16[128,1,8192]{2,1,0:T(2,128)(2,1)}) %all-gather.7.cloned.1.call-update) | async-done | bytes 2097168 | tf_op jit(solution)/shard_map/all_gather | solution.py:141
  404.9 12.6 %reduce.3 = bf16[128,8192]{1,0:T(8,128)(2,1)S(1)} reduce(bf16[128,1,8192]{2,1,0:T(2,128)(2,1)} %all-gather.7.cloned.1.call-done, bf16[]{:T(256)} %constant.249), dimensions={1}, to_apply=%all-gather.1.reduce_sub_computation | reduce | bytes 4194306 | tf_op jit(solution)/shard_map/all_gather | solution.py:141
  422.4 7.8 %fusion.40 = f32[4,64,1,128]{3,2,1,0:T(1,128)S(1)} fusion(bf16[4,64,128,128]{3,2,1,0:T(8,128)(2,1)} %param.14, bf16[4,64,128,1]{2,1,0,3:T(8,128)(2,1)S(1)} %bitcast.178), kind=kOutput, calls=%fused_computation.69 | convolution fusion | flops 8388608 | bytes 8585216 | tf_op jit(solution)/shard_map/dtsp,dtp->dts/dot_general | solution.py:143
  430.3 5.7 fusion.38
  439.6 4.9 reshape.523
  444.6 35.7 %while.29 = (s32[]{:T(128)}, f32[2,8,128]{2,0,1:T(2,128)S(1)}, s32[8]{0:T(128)S(1)}, bf16[8,6144,128]{2,1,0:T(8,128)(2,1)}, bf16[2,8,128]{2,0,1:T(2,128)(2,1)S(1...) while((s32[]{:T(128)}, f32[2,8,128]{2,0,1:T(2,128)S(1)}, ...), condition=%wide.region_11.12_spmd.clone, body=%wide.region_10.11_spmd.clone.sunk | while | flops 4227591 | bytes 2137796 | solution.py:78
  480.4 15.8 %all_to_all.66 = f32[2,8,128]{1,0,2:T(2,128)S(1)} all-to-all(f32[2,8,128]{1,0,2:T(2,128)S(1)} %copy.55), channel_id=1, replica_groups=mesh['det'=8,'tm'=16] {'det','tm'}, dimensions={2} | all-to-all | bytes 16384 | tf_op jit(solution)/shard_map/all_to_all | solution.py:101
  508.1 88.1 %all-reduce.8.cloned.1.call-done = f32[128,8192]{1,0:T(8,128)} async-done(((f32[128,8192]{1,0:T(8,128)}), f32[128,8192]{1,0:T(8,128)}) %all-reduce.8.cloned.1.call-update) | async-done | bytes 4194320
  (199 shorter events, 131.4 us)
Async XLA Ops:
  11.6 13.0 %copy-start.1 = (s32[1024]{0:T(1024)S(1)}, s32[1024]{0:T(1024)}, u32[]{:S(2)}) copy-start(s32[1024]{0:T(1024)} %param.20) | copy-start | bytes 12292
  11.6 25.8 %copy-start.2 = (f32[1,8192]{1,0:T(1,128)S(1)}, f32[1,8192]{1,0:T(1,128)}, u32[]{:S(2)}) copy-start(f32[1,8192]{1,0:T(1,128)} %param.17) | copy-start | bytes 98308
  11.7 26.6 %copy-start.3 = (s32[4,64]{1,0:T(4,128)S(1)}, s32[4,64]{1,0:T(4,128)}, u32[]{:S(2)}) copy-start(s32[4,64]{1,0:T(4,128)} %param.15) | copy-start | bytes 3076
  11.7 26.7 %copy-start.4 = (f32[4]{0:T(128)S(1)}, f32[4]{0:T(128)}, u32[]{:S(2)}) copy-start(f32[4]{0:T(128)} %param.16) | copy-start | bytes 52
  25.9 83.3 %all-to-all-start = ((bf16[2,1024,1]{2,0,1:T(2,128)(2,1)}), bf16[2,1024,1]{2,0,1:T(2,128)(2,1)S(1)}, u32[]{:S(2)}, u32[]{:S(2)}) async-start(bf16[2,1024,1]{2,0,1:T(2,128)(2,1)} %copy.46), calls=%async_computation | async-start | bytes 1048576 | tf_op jit(solution)/shard_map/all_to_all | solution.py:99
  37.4 107.9 %all-gather.5.cloned.1.call-start = ((), (), s32[]{:S(2)}) async-start(), calls=%async_computation.4 | async-start | bytes 4227072 | tf_op jit(solution)/shard_map/all_gather | solution.py:141
  38.2 297.8 %all-reduce.6.cloned.1.call-start = ((), (), s32[]{:S(2)}) async-start(), calls=%async_computation.6 | async-start | bytes 8388608
  162.9 7.8 %copy-start = (f32[4,64,128]{2,1,0:T(8,128)S(1)}, f32[4,64,128]{2,1,0:T(8,128)}, u32[]{:S(2)}) copy-start(f32[4,64,128]{2,1,0:T(8,128)} %param.13) | copy-start | bytes 393220
  185.8 15.0 %all-to-all-start.1 = ((f32[2,8,128]{1,0,2:T(2,128)}), f32[2,8,128]{1,0,2:T(2,128)S(1)}, u32[]{:S(2)}, u32[]{:S(2)}) async-start(f32[2,8,128]{1,0,2:T(2,128)} %copy.50), calls=%async_computation.1 | async-start | bytes 262144 | tf_op jit(solution)/shard_map/all_to_all | solution.py:101
  190.6 214.3 %all-gather.7.cloned.1.call-start = ((), (), s32[]{:S(2)}) async-start(), calls=%async_computation.5 | async-start | bytes 4227072 | tf_op jit(solution)/shard_map/all_gather | solution.py:141
  354.2 20.6 %all-to-all-start.2 = ((bf16[2,1024,1]{2,0,1:T(2,128)(2,1)}), bf16[2,1024,1]{2,0,1:T(2,128)(2,1)S(1)}, u32[]{:S(2)}, u32[]{:S(2)}) async-start(bf16[2,1024,1]{2,0,1:T(2,128)(2,1)} %copy.51), calls=%async_computation.2 | async-start | bytes 1048576 | tf_op jit(solution)/shard_map/all_to_all | solution.py:99
  360.8 235.5 %all-reduce.8.cloned.1.call-start = ((), (), s32[]{:S(2)}) async-start(), calls=%async_computation.7 | async-start | bytes 8388608
Sparse Core Ops, SparseCore 0:
  41.4 68.8 all-gather.4
  185.2 150.7 all-reduce.5
  339.2 65.6 all-gather.6
  444.7 151.5 all-reduce.7
where the time goes:
time: 611 us; the launch traced here: 605 us
  waiting for transfers between devices  265 us (43%)
  matrix products  89.6 us (15%)
  local copies, waits for them, and re-layouts  86.5 us (14%)
  blocking collectives  84.3 us (14%)
  other arithmetic  41.5 us (7%)
  starting transfers between devices  23.2 us (4%)
  between operations  14.5 us (2%)
    unnamed x6, waiting for transfers between devices  211 us
    unnamed x1, blocking collectives  68.5 us
    dot_general x24, matrix products, one_block(): jnp.einsum('mlr,cml->cmr', table, scaled, preferred_element_type=jnp.floa...  50.4 us
    all_gather x2, waiting for transfers between devices, on_device(): lax.all_gather(map_half, ('det', 'tm'), axis=0, tiled=True)  29.4 us
    all_gather x2, other arithmetic, on_device(): lax.all_gather(map_half, ('det', 'tm'), axis=0, tiled=True)  25.2 us
    dynamic_slice x24, local copies, waits for them, and re-layouts, one_block(): gain_block = lax.dynamic_slice_in_dim(prior_gain, start, block_rows)  18.3 us
    all_to_all x2, starting transfers between devices, harmonic_filter(): lax.all_to_all(outward, ('det', 'tm'), split_axis=1, concat_axis=2, tiled...  18.1 us
    scatter x4, local copies, waits for them, and re-layouts, harmonic_filter(): jnp.zeros((cycles_here, length), jnp.float32).at[:, spectrum_slot]  17.6 us
  transfers between devices with their start and end apart: 7, of which 5 were waited for; matrix products, arithmetic and copies ran while one was open for 19% of the time, Pallas kernels for 0%

commit v1 on v0

--- a/solution.py
+++ b/solution.py
@@ -138,7 +138,11 @@
     current = start_map
     for iteration in range(ITERS):
         map_half = current.astype(jnp.bfloat16)
-        gathered = lax.all_gather(map_half, ("det", "tm"), axis=0, tiled=True).reshape(nblocks, 128)
+        take_fields_here = lambda patch, peer_axis, dim_no: jnp.concatenate(
+            lax.all_to_all(jnp.stack([patch] * lax.axis_size(peer_axis), 0), peer_axis, 0, 0),
+            dim_no,
+        )
+        gathered = take_fields_here(map_half, ("det", "tm"), 0).reshape(nblocks, 128)
         picked = gathered[pix_block]
         predicted = jnp.einsum(
             "dtsp,dtp->dts", pointing, picked, preferred_element_type=jnp.float32

time: 611 us -> 676 us (1.11)
  local copies, waits for them, and re-layouts: 86.5 us -> 119 us
  other arithmetic: 41.5 us -> 66.8 us
  starting transfers between devices: 23.2 us -> 42.4 us
  waiting for transfers between devices: 265 us -> 250 us
    all_gather x2 -> x0, waiting for transfers between devices: 29.4 us -> none  [on_device(): lax.all_gather(map_half, ('det', 'tm'), axis=0, tiled=True)]
    all_to_all x0 -> x2, waiting for transfers between devices: none -> 28.6 us  [on_device(): lax.all_to_all(jnp.stack([patch] * lax.axis_size(peer_axis), 0), peer_axi...]
    another operation x2 -> x4, other arithmetic: 0.11 us -> 26.5 us  [the longest x2 26.4 us: on_device(): jnp.stack([patch] * lax.axis_size(peer_axis), 0)]
    all_gather x2 -> x0, other arithmetic: 25.2 us -> none  [on_device(): lax.all_gather(map_half, ('det', 'tm'), axis=0, tiled=True)]
    all_to_all x0 -> x2, other arithmetic: none -> 25.2 us  [on_device(): lax.all_to_all(jnp.stack([patch] * lax.axis_size(peer_axis), 0), peer_axi...]
    unnamed x12 -> x16, local copies, waits for them, and re-layouts: 0.21 us -> 19.3 us
    another operation x0 -> x5, local copies, waits for them, and re-layouts: none -> 17.5 us  [the longest x3 12.8 us: on_device(): jnp.stack([patch] * lax.axis_size(peer_axis), 0)]
    all_to_all x0 -> x2, starting transfers between devices: none -> 14.5 us  [on_device(): lax.all_to_all(jnp.stack([patch] * lax.axis_size(peer_axis), 0), peer_axi...]
  transfers between devices with their start and end apart: 7 -> 7, of which waited for: 5 -> 4; matrix products, arithmetic and copies ran while one was open for 19% -> 22% of each run, Pallas kernels for 0% -> 0%
where the time goes in v1:
time: 676 us; the launch traced here: 665 us
  waiting for transfers between devices  250 us (37%)
  local copies, waits for them, and re-layouts  119 us (18%)
  matrix products  89.6 us (13%)
  blocking collectives  83.2 us (12%)
  other arithmetic  66.8 us (10%)
  starting transfers between devices  42.4 us (6%)
  between operations  14.8 us (2%)
    unnamed x4, waiting for transfers between devices  211 us
    unnamed x1, blocking collectives  67.4 us
    dot_general x24, matrix products, one_block(): jnp.einsum('mlr,cml->cmr', table, scaled, preferred_element_type=jnp.floa...  50.4 us
    all_to_all x2, waiting for transfers between devices, on_device(): lax.all_to_all(jnp.stack([patch] * lax.axis_size(peer_axis), 0), peer_axi...  28.6 us
    another operation x2, other arithmetic, on_device(): jnp.stack([patch] * lax.axis_size(peer_axis), 0)  26.4 us
    all_to_all x2, other arithmetic, on_device(): lax.all_to_all(jnp.stack([patch] * lax.axis_size(peer_axis), 0), peer_axi...  25.2 us
    unnamed x16, local copies, waits for them, and re-layouts  19.3 us
    dynamic_slice x24, local copies, waits for them, and re-layouts, one_block(): gain_block = lax.dynamic_slice_in_dim(prior_gain, start, block_rows)  18.4 us
  transfers between devices with their start and end apart: 7, of which 4 were waited for; matrix products, arithmetic and copies ran while one was open for 22% of the time, Pallas kernels for 0%

profile of v1, /device:TPU:1, one launch (start us, length us, event | category | flops | bytes accessed | tf_op | source)
XLA Modules:
  0.0 665.5 jit_solution(4751317596054363744)
XLA Ops:
  11.7 6.2 gather_fusion.1
  17.8 6.2 gather_fusion.2
  25.9 11.5 %all-to-all-start.1 = ((bf16[2,1024,1]{2,0,1:T(2,128)(2,1)}), bf16[2,1024,1]{2,0,1:T(2,128)(2,1)S(1)}, u32[]{:S(2)}, u32[]{:S(2)}) async-start(bf16[2,1024,1]{2,0,1:T(2,128)(2,1)} %copy.46), calls=%async_computation.1 | async-start | bytes 1048576 | tf_op jit(solution)/shard_map/all_to_all | solution.py:99
  39.9 67.4 %all-reduce.1 = f32[128,64]{1,0:T(8,128)S(1)} all-reduce(f32[128,64]{1,0:T(8,128)S(1)} %reshape.519), channel_id=3, replica_groups=mesh['det'=8,'tm'=16] {'det','tm'}, use_global_device_ids=true, to_apply=%region_7.8.clone | all-reduce | flops 8192 | bytes 65536
  114.1 13.2 %reduce.22 = bf16[128,8192]{1,0:T(8,128)(2,1)S(1)} reduce(bf16[128,1,8192]{2,1,0:T(2,128)(2,1)} %stack.16, bf16[]{:T(256)} %broadcast.847), dimensions={1}, to_apply=%stack.16.reduce_sub_computation | reduce | bytes 4194306 | tf_op jit(solution)/shard_map/stack | solution.py:142
  135.5 35.5 %while.28 = (s32[]{:T(128)}, f32[2,8,128]{2,0,1:T(2,128)S(1)}, s32[8]{0:T(128)S(1)}, bf16[8,6144,128]{2,1,0:T(8,128)(2,1)}, bf16[2,8,128]{2,0,1:T(2,128)(2,1)S(1...) while((s32[]{:T(128)}, f32[2,8,128]{2,0,1:T(2,128)S(1)}, ...), condition=%wide.region_3.0_spmd.clone, body=%wide.region_2.0_spmd.clone.sunk | while | flops 4227591 | bytes 2137796 | solution.py:78
  171.0 6.8 %reshape.726 = bf16[128,1,8192]{2,1,0:T(2,128)(2,1)} reshape(bf16[128,2,4096]{2,1,0:T(2,128)(2,1)S(1)} %all-to-all-done) | data formatting | bytes 4194304
  177.8 12.6 %reduce.1 = bf16[128,8192]{1,0:T(8,128)(2,1)S(1)} reduce(bf16[128,1,8192]{2,1,0:T(2,128)(2,1)} %reshape.726, bf16[]{:T(256)} %constant.249), dimensions={1}, to_apply=%all_to_all.54.reduce_sub_computation | reduce | bytes 4194306 | tf_op jit(solution)/shard_map/all_to_all | solution.py:142
  195.3 7.8 %fusion.44 = f32[4,64,1,128]{3,2,1,0:T(1,128)S(1)} fusion(bf16[4,64,128,128]{3,2,1,0:T(8,128)(2,1)} %param.14, bf16[4,64,128,1]{2,1,0,3:T(8,128)(2,1)S(1)} %bitcast.175), kind=kOutput, calls=%fused_computation.73 | convolution fusion | flops 8388608 | bytes 8585216 | tf_op jit(solution)/shard_map/dtsp,dtp->dts/dot_general | solution.py:147
  218.3 9.8 %all-to-all-start.2 = ((f32[2,8,128]{1,0,2:T(2,128)}), f32[2,8,128]{1,0,2:T(2,128)S(1)}, u32[]{:S(2)}, u32[]{:S(2)}) async-start(f32[2,8,128]{1,0,2:T(2,128)} %copy.50), calls=%async_computation.2 | async-start | bytes 262144 | tf_op jit(solution)/shard_map/all_to_all | solution.py:101
  228.1 10.2 %all-to-all-done.2 = f32[2,8,128]{1,0,2:T(2,128)S(1)} async-done(((f32[2,8,128]{1,0,2:T(2,128)}), f32[2,8,128]{1,0,2:T(2,128)S(1)}, u32[]{:S(2)}, u32[]{:S(2)}) %all-to-all-start.2) | async-done | bytes 8224 | tf_op jit(solution)/shard_map/all_to_all | solution.py:101
  250.5 123.0 %all-reduce.6.cloned.1.call-done = f32[128,8192]{1,0:T(8,128)} async-done(((f32[128,8192]{1,0:T(8,128)}), f32[128,8192]{1,0:T(8,128)}) %all-reduce.6.cloned.1.call-update) | async-done | bytes 4194320
  376.9 6.2 gather_fusion.4
  383.7 6.2 gather_fusion.5
  391.1 6.6 all-to-all-start.4
  403.8 13.2 %reduce.23 = bf16[128,8192]{1,0:T(8,128)(2,1)S(1)} reduce(bf16[128,1,8192]{2,1,0:T(2,128)(2,1)} %stack.20, bf16[]{:T(256)} %broadcast.847), dimensions={1}, to_apply=%stack.20.reduce_sub_computation | reduce | bytes 4194306 | tf_op jit(solution)/shard_map/stack | solution.py:142
  419.8 9.8 %all-to-all-start.3 = ((bf16[128,2,4096]{2,1,0:T(2,128)(2,1)}), bf16[128,2,4096]{2,1,0:T(2,128)(2,1)S(1)}, u32[]{:S(2)}, u32[]{:S(2)}) async-start(bf16[128,2,4096]{2,1,0:T(2,128)(2,1)} %reshape.727), calls=%async_computation.3 | async-start | bytes 4194304 | tf_op jit(solution)/shard_map/all_to_all | solution.py:142
  430.2 28.6 %all-to-all-done.3 = bf16[128,2,4096]{2,1,0:T(2,128)(2,1)S(1)} async-done(((bf16[128,2,4096]{2,1,0:T(2,128)(2,1)}), bf16[128,2,4096]{2,1,0:T(2,128)(2,1)S(1)}, u32[]{:S(2)}, u32[]{:S(2)}) %all-to-all-start.3) | async-done | bytes 2097184 | tf_op jit(solution)/shard_map/all_to_all | solution.py:142
  458.8 6.8 %reshape.728 = bf16[128,1,8192]{2,1,0:T(2,128)(2,1)} reshape(bf16[128,2,4096]{2,1,0:T(2,128)(2,1)S(1)} %all-to-all-done.3) | data formatting | bytes 4194304
  465.6 12.6 %reduce.5 = bf16[128,8192]{1,0:T(8,128)(2,1)S(1)} reduce(bf16[128,1,8192]{2,1,0:T(2,128)(2,1)} %reshape.728, bf16[]{:T(256)} %constant.249), dimensions={1}, to_apply=%all_to_all.62.reduce_sub_computation | reduce | bytes 4194306 | tf_op jit(solution)/shard_map/all_to_all | solution.py:142
  483.2 7.8 %fusion.40 = f32[4,64,1,128]{3,2,1,0:T(1,128)S(1)} fusion(bf16[4,64,128,128]{3,2,1,0:T(8,128)(2,1)} %param.14, bf16[4,64,128,1]{2,1,0,3:T(8,128)(2,1)S(1)} %bitcast.174), kind=kOutput, calls=%fused_computation.69 | convolution fusion | flops 8388608 | bytes 8585216 | tf_op jit(solution)/shard_map/dtsp,dtp->dts/dot_general | solution.py:147
  505.3 35.7 %while.29 = (s32[]{:T(128)}, f32[2,8,128]{2,0,1:T(2,128)S(1)}, s32[8]{0:T(128)S(1)}, bf16[8,6144,128]{2,1,0:T(8,128)(2,1)}, bf16[2,8,128]{2,0,1:T(2,128)(2,1)S(1...) while((s32[]{:T(128)}, f32[2,8,128]{2,0,1:T(2,128)S(1)}, ...), condition=%wide.region_11.12_spmd.clone, body=%wide.region_10.11_spmd.clone.sunk | while | flops 4227591 | bytes 2137796 | solution.py:78
  541.2 15.7 %all_to_all.76 = f32[2,8,128]{1,0,2:T(2,128)S(1)} all-to-all(f32[2,8,128]{1,0,2:T(2,128)S(1)} %copy.55), channel_id=1, replica_groups=mesh['det'=8,'tm'=16] {'det','tm'}, dimensions={2} | all-to-all | bytes 16384 | tf_op jit(solution)/shard_map/all_to_all | solution.py:101
  569.0 87.8 %all-reduce.8.cloned.1.call-done = f32[128,8192]{1,0:T(8,128)} async-done(((f32[128,8192]{1,0:T(8,128)}), f32[128,8192]{1,0:T(8,128)}) %all-reduce.8.cloned.1.call-update) | async-done | bytes 4194320
  (206 shorter events, 174.5 us)
Async XLA Ops:
  11.6 13.0 %copy-start.1 = (s32[1024]{0:T(1024)S(1)}, s32[1024]{0:T(1024)}, u32[]{:S(2)}) copy-start(s32[1024]{0:T(1024)} %param.20) | copy-start | bytes 12292
  11.6 25.8 %copy-start.2 = (f32[1,8192]{1,0:T(1,128)S(1)}, f32[1,8192]{1,0:T(1,128)}, u32[]{:S(2)}) copy-start(f32[1,8192]{1,0:T(1,128)} %param.17) | copy-start | bytes 98308
  11.7 25.9 %copy-start.3 = (s32[4,64]{1,0:T(4,128)S(1)}, s32[4,64]{1,0:T(4,128)}, u32[]{:S(2)}) copy-start(s32[4,64]{1,0:T(4,128)} %param.15) | copy-start | bytes 3076
  11.7 26.0 %copy-start.4 = (f32[4]{0:T(128)S(1)}, f32[4]{0:T(128)}, u32[]{:S(2)}) copy-start(f32[4]{0:T(128)} %param.16) | copy-start | bytes 52
  25.9 104.2 %all-to-all-start.1 = ((bf16[2,1024,1]{2,0,1:T(2,128)(2,1)}), bf16[2,1024,1]{2,0,1:T(2,128)(2,1)S(1)}, u32[]{:S(2)}, u32[]{:S(2)}) async-start(bf16[2,1024,1]{2,0,1:T(2,128)(2,1)} %copy.46), calls=%async_computation.1 | async-start | bytes 1048576 | tf_op jit(solution)/shard_map/all_to_all | solution.py:99
  130.1 40.9 %all-to-all-start = ((bf16[128,2,4096]{2,1,0:T(2,128)(2,1)}), bf16[128,2,4096]{2,1,0:T(2,128)(2,1)S(1)}, u32[]{:S(2)}, u32[]{:S(2)}) async-start(bf16[128,2,4096]{2,1,0:T(2,128)(2,1)} %reshape.725), calls=%async_computation | async-start | bytes 4194304 | tf_op jit(solution)/shard_map/all_to_all | solution.py:142
  134.8 238.6 %all-reduce.6.cloned.1.call-start = ((), (), s32[]{:S(2)}) async-start(), calls=%async_computation.6 | async-start | bytes 8388608
  195.3 7.8 %copy-start = (f32[4,64,128]{2,1,0:T(8,128)S(1)}, f32[4,64,128]{2,1,0:T(8,128)}, u32[]{:S(2)}) copy-start(f32[4,64,128]{2,1,0:T(8,128)} %param.13) | copy-start | bytes 393220
  218.3 20.0 %all-to-all-start.2 = ((f32[2,8,128]{1,0,2:T(2,128)}), f32[2,8,128]{1,0,2:T(2,128)S(1)}, u32[]{:S(2)}, u32[]{:S(2)}) async-start(f32[2,8,128]{1,0,2:T(2,128)} %copy.50), calls=%async_computation.2 | async-start | bytes 262144 | tf_op jit(solution)/shard_map/all_to_all | solution.py:101
  391.1 28.7 %all-to-all-start.4 = ((bf16[2,1024,1]{2,0,1:T(2,128)(2,1)}), bf16[2,1024,1]{2,0,1:T(2,128)(2,1)S(1)}, u32[]{:S(2)}, u32[]{:S(2)}) async-start(bf16[2,1024,1]{2,0,1:T(2,128)(2,1)} %copy.51), calls=%async_computation.4 | async-start | bytes 1048576 | tf_op jit(solution)/shard_map/all_to_all | solution.py:99
  419.8 39.0 %all-to-all-start.3 = ((bf16[128,2,4096]{2,1,0:T(2,128)(2,1)}), bf16[128,2,4096]{2,1,0:T(2,128)(2,1)S(1)}, u32[]{:S(2)}, u32[]{:S(2)}) async-start(bf16[128,2,4096]{2,1,0:T(2,128)(2,1)} %reshape.727), calls=%async_computation.3 | async-start | bytes 4194304 | tf_op jit(solution)/shard_map/all_to_all | solution.py:142
  429.6 227.2 %all-reduce.8.cloned.1.call-start = ((), (), s32[]{:S(2)}) async-start(), calls=%async_computation.7 | async-start | bytes 8388608
Sparse Core Ops, SparseCore 0:
  217.6 155.7 all-reduce.5
  505.4 151.3 all-reduce.7
